TPU v7x, 512 devices: a whole 4x4x16 slice. The times are simulated.
512 devices in a mesh: band: 32 (over y, x, z_hi), slab: 16 (over z_lo, core).
Axes of the slice: x: 4, y: 4, z: 16 (z_hi: 2, z_lo: 8; z = z_hi * 8 + z_lo), core: 2. Of those that a mesh axis runs over, the one named last changes fastest.
Arguments:
- wave_coeffs: float32 [64, 2, 128, 128, 128], P('band', None, 'slab'), may hold values from -12 to 12
- column_mask: int32 [128, 128], replicated, may hold values from 0 to 1, as said below
- occupations: float32 [64], P('band'), may hold values from 0.1 to 2
- core_density: float32 [128, 128, 128], P('band', 'slab'), may hold values from 0.05 to 0.5
Outputs:
- hartree: float32 [128, 128, 128], P('band', 'slab')
- xc_potential: float32 [128, 128, 128], P('band', 'slab')
Inputs may be any that keep to these rules, and one draw needn't show every extreme that they name: `column_mask`: 1 marks a column of frequencies (first two indices) inside the cutoff; only columns whose shifted indices s1, s2 satisfy s1^2 + s2^2 <= 32^2 can be 1.
All inputs are finite; a program needn't handle non-finite values.
Results may differ from a plain program's by a relative error of at most 0.00035.
Values sent between devices are 32-bit elements; how exact they have to be, the bound alone decides.
No kernel may reach another device: no remote copies, remote signals or barrier semaphores. Data moves between devices by JAX's collectives and lax.ppermute only.
A program may use at most 64 MiB of HBM per device.

v0:
```python
import math
import jax
import jax.numpy as jnp
from jax import lax
from jax.sharding import PartitionSpec as P

grid_spacing = 0.59
wigner_a = 0.44
wigner_b = 7.8


def dft_tables(extent):
    indices = jnp.arange(extent, dtype=jnp.int32)
    phase = indices[:, None] * indices[None, :] % extent
    angle = phase.astype(jnp.float32) * (2.0 * math.pi / extent)
    return (jnp.cos(angle), jnp.sin(angle))


def kernel_block(extent, starts, amounts):
    pieces = []
    for offset, amount in zip(starts, amounts):
        frequency = offset + jnp.arange(amount, dtype=jnp.int32)
        shifted = (frequency + extent // 2) % extent - extent // 2
        pieces.append(shifted * shifted)
    squared = pieces[0][:, None, None] + pieces[1][None, :, None] + pieces[2][None, None, :]
    length = extent * grid_spacing
    scaled = length * length / math.pi / jnp.maximum(squared, 1).astype(jnp.float32)
    return jnp.where(squared == 0, 0.0, scaled)


def exchange_correlation(density):
    root_density = jnp.cbrt(density)
    radius = (3.0 / (4.0 * math.pi)) ** (1.0 / 3.0) / root_density
    exchange_part = -((3.0 / math.pi) ** (1.0 / 3.0)) * root_density
    shifted = radius + wigner_b
    correlation = -wigner_a / shifted - wigner_a * radius / (3.0 * shifted * shifted)
    return exchange_part + correlation


def project(pattern, values, matrix):
    return jnp.einsum(pattern, values, matrix, precision=lax.Precision.HIGHEST)


def rotate(real_part, imag_part, pattern, cosine_table, sine_table, direction):
    new_real = project(pattern, real_part, cosine_table) - direction * project(
        pattern, imag_part, sine_table
    )
    new_imag = direction * project(pattern, real_part, sine_table) + project(
        pattern, imag_part, cosine_table
    )
    return (new_real, new_imag)


def local(wave_coeffs, column_mask, occupations, core_density):
    local_bands = wave_coeffs.shape[0]
    row_count = wave_coeffs.shape[2]
    extent = wave_coeffs.shape[3]
    bands_all = lax.axis_size("band") * local_bands
    band_rows = extent // lax.axis_size("band")
    slab_index = lax.axis_index("slab")
    band_index = lax.axis_index("band")
    cosine_table, sine_table = dft_tables(extent)
    mask_rows = lax.dynamic_slice_in_dim(column_mask, slab_index * row_count, row_count, 0).astype(
        jnp.float32
    )
    masked = wave_coeffs * mask_rows[None, None, :, :, None]
    real_part, imag_part = rotate(
        masked[:, 0], masked[:, 1], "bxyz,zw->bxyw", cosine_table, sine_table, 1.0
    )
    real_part, imag_part = rotate(
        real_part, imag_part, "bxyz,yw->bxwz", cosine_table, sine_table, 1.0
    )
    stacked = jnp.stack((real_part, imag_part), axis=1)
    factor = 1.0 / (float(extent) ** 3 * bands_all)
    partial_value = jnp.zeros((extent, row_count, extent), jnp.float32)
    for member in range(local_bands):
        arrived = lax.all_to_all(stacked[member], "slab", split_axis=2, concat_axis=1, tiled=True)
        plane_real, plane_imag = rotate(
            arrived[0], arrived[1], "xyz,xw->wyz", cosine_table, sine_table, 1.0
        )
        partial_value = partial_value + occupations[member] * (
            plane_real * plane_real + plane_imag * plane_imag
        )
    partial_value = partial_value * factor
    density = lax.psum(partial_value, "band")
    own_density = lax.dynamic_slice_in_dim(density, band_index * band_rows, band_rows, 0)
    first_real = project("xyz,zw->xyw", density, cosine_table)
    first_imag = -project("xyz,zw->xyw", density, sine_table)
    line_real, line_imag = rotate(
        first_real, first_imag, "xyz,xw->wyz", cosine_table, sine_table, -1.0
    )
    arrived = lax.all_to_all(
        jnp.stack((line_real, line_imag)), "slab", split_axis=1, concat_axis=2, tiled=True
    )
    line_real, line_imag = rotate(
        arrived[0], arrived[1], "xyz,yw->xwz", cosine_table, sine_table, -1.0
    )
    kernel = kernel_block(extent, (slab_index * row_count, 0, 0), (row_count, extent, extent))
    line_real, line_imag = rotate(
        kernel * line_real, kernel * line_imag, "xyz,yw->xwz", cosine_table, sine_table, 1.0
    )
    arrived = lax.all_to_all(
        jnp.stack((line_real, line_imag)), "slab", split_axis=2, concat_axis=1, tiled=True
    )
    cosine_rows = lax.dynamic_slice_in_dim(cosine_table, band_index * band_rows, band_rows, 1)
    sine_rows = lax.dynamic_slice_in_dim(sine_table, band_index * band_rows, band_rows, 1)
    line_real, line_imag = rotate(
        arrived[0], arrived[1], "xyz,xw->wyz", cosine_rows, sine_rows, 1.0
    )
    spatial = project("xyz,zw->xyw", line_real, cosine_table) - project(
        "xyz,zw->xyw", line_imag, sine_table
    )
    hartree = spatial / float(extent) ** 3
    xc_potential = exchange_correlation(own_density + core_density)
    return (hartree, xc_potential)


def solution(mesh):
    return jax.shard_map(
        local,
        mesh=mesh,
        in_specs=(P("band", None, "slab", None, None), P(), P("band"), P("band", "slab", None)),
        out_specs=(P("band", "slab", None), P("band", "slab", None)),
        check_vma=False,
    )
```

profile of v0, /device:TPU:65, one launch (start us, length us, event | category | flops | bytes accessed | tf_op | source)
XLA Modules:
  0.0 862.5 jit_solution(3773633972059874277)
XLA Ops:
  7.9 1.9 copy_multiply_fusion
  9.7 1.2 fusion.26
  12.2 1.2 convolution_subtract_fusion.1
  13.4 1.3 fusion.61
  14.7 1.3 fusion.64
  16.0 1.2 convolution_add_fusion.1
  17.2 1.3 fusion.1
  18.6 1.3 fusion
  20.1 1.6 copy.102
  21.7 12.5 %all-to-all-start = ((f32[2,8,128,128]{3,1,0,2:T(8,128)}), f32[2,8,128,128]{3,1,0,2:T(8,128)S(1)}, u32[]{:S(2)}, u32[]{:S(2)}) async-start(f32[2,8,128,128]{3,1,0,2:T(8,128)} %copy.102), calls=%async_computation | async-start | bytes 2097152 | tf_op jit(solution)/shard_map/all_to_all | solution.py:77
  34.2 1.6 copy.104
  35.8 47.0 %all-to-all-done = f32[2,8,128,128]{3,1,0,2:T(8,128)S(1)} async-done(((f32[2,8,128,128]{3,1,0,2:T(8,128)}), f32[2,8,128,128]{3,1,0,2:T(8,128)S(1)}, u32[]{:S(2)}, u32[]{:S(2)}) %all-to-all-start) | async-done | bytes 1048608 | tf_op jit(solution)/shard_map/all_to_all | solution.py:77
  82.8 6.7 all-to-all-start.1
  92.1 46.0 %all-to-all-done.1 = f32[2,8,128,128]{3,1,0,2:T(8,128)S(1)} async-done(((f32[2,8,128,128]{3,1,0,2:T(8,128)}), f32[2,8,128,128]{3,1,0,2:T(8,128)S(1)}, u32[]{:S(2)}, u32[]{:S(2)}) %all-to-all-start.1) | async-done | bytes 1048608 | tf_op jit(solution)/shard_map/all_to_all | solution.py:77
  141.6 1.6 fusion.19
  143.2 2.4 fusion.21
  145.6 554.2 %all-reduce.2.cloned.1.call-done = f32[128,8,128]{2,0,1:T(8,128)} async-done(((f32[128,8,128]{2,0,1:T(8,128)}), f32[128,8,128]{2,0,1:T(8,128)}) %all-reduce.2.cloned.1.call-update) | async-done | bytes 524304 | tf_op jit(solution)/shard_map/psum | solution.py:85
  699.8 1.9 fusion.70
  706.1 1.6 copy.108
  707.7 31.5 %all-to-all-start.2 = ((f32[2,128,8,128]{3,2,0,1:T(8,128)}), f32[2,128,8,128]{3,2,0,1:T(8,128)S(1)}, u32[]{:S(2)}, u32[]{:S(2)}) async-start(f32[2,128,8,128]{3,2,0,1:T(8,128)} %copy.108), calls=%async_computation.2 | async-start | bytes 2097152 | tf_op jit(solution)/shard_map/all_to_all | solution.py:92
  739.3 48.5 %all-to-all-done.2 = f32[2,128,8,128]{3,2,0,1:T(8,128)S(1)} async-done(((f32[2,128,8,128]{3,2,0,1:T(8,128)}), f32[2,128,8,128]{3,2,0,1:T(8,128)S(1)}, u32[]{:S(2)}, u32[]{:S(2)}) %all-to-all-start.2) | async-done | bytes 1048608 | tf_op jit(solution)/shard_map/all_to_all | solution.py:92
  795.0 1.6 copy.110
  796.6 6.7 all-to-all-start.3
  804.5 47.4 %all-to-all-done.3 = f32[2,8,128,128]{3,1,0,2:T(8,128)S(1)} async-done(((f32[2,8,128,128]{3,1,0,2:T(8,128)}), f32[2,8,128,128]{3,1,0,2:T(8,128)S(1)}, u32[]{:S(2)}, u32[]{:S(2)}) %all-to-all-start.3) | async-done | bytes 1048608 | tf_op jit(solution)/shard_map/all_to_all | solution.py:102
  (53 shorter events, 24.7 us)
Async XLA Ops:
  21.7 61.1 %all-to-all-start = ((f32[2,8,128,128]{3,1,0,2:T(8,128)}), f32[2,8,128,128]{3,1,0,2:T(8,128)S(1)}, u32[]{:S(2)}, u32[]{:S(2)}) async-start(f32[2,8,128,128]{3,1,0,2:T(8,128)} %copy.102), calls=%async_computation | async-start | bytes 2097152 | tf_op jit(solution)/shard_map/all_to_all | solution.py:77
  34.2 55.5 %copy-start.2 = (f32[2]{0:T(128)S(1)}, f32[2]{0:T(128)}, u32[]{:S(2)}) copy-start(f32[2]{0:T(128)} %param.6) | copy-start | bytes 28
  82.8 55.3 %all-to-all-start.1 = ((f32[2,8,128,128]{3,1,0,2:T(8,128)}), f32[2,8,128,128]{3,1,0,2:T(8,128)S(1)}, u32[]{:S(2)}, u32[]{:S(2)}) async-start(f32[2,8,128,128]{3,1,0,2:T(8,128)} %copy.104), calls=%async_computation.1 | async-start | bytes 2097152 | tf_op jit(solution)/shard_map/all_to_all | solution.py:77
  89.5 610.3 %all-reduce.2.cloned.1.call-start = ((), (), s32[]{:S(2)}) async-start(), calls=%async_computation.4 | async-start | bytes 1048576 | tf_op jit(solution)/shard_map/psum | solution.py:85
  699.8 3.6 copy-start
  707.7 80.1 %all-to-all-start.2 = ((f32[2,128,8,128]{3,2,0,1:T(8,128)}), f32[2,128,8,128]{3,2,0,1:T(8,128)S(1)}, u32[]{:S(2)}, u32[]{:S(2)}) async-start(f32[2,128,8,128]{3,2,0,1:T(8,128)} %copy.108), calls=%async_computation.2 | async-start | bytes 2097152 | tf_op jit(solution)/shard_map/all_to_all | solution.py:92
  795.0 8.8 %copy-start.1 = (f32[4,8,128]{2,1,0:T(8,128)S(1)}, f32[4,8,128]{2,1,0:T(8,128)}, u32[]{:S(2)}) copy-start(f32[4,8,128]{2,1,0:T(8,128)} %param.7) | copy-start | bytes 49156
  796.6 55.3 %all-to-all-start.3 = ((f32[2,8,128,128]{3,1,0,2:T(8,128)}), f32[2,8,128,128]{3,1,0,2:T(8,128)S(1)}, u32[]{:S(2)}, u32[]{:S(2)}) async-start(f32[2,8,128,128]{3,1,0,2:T(8,128)} %copy.110), calls=%async_computation.3 | async-start | bytes 2097152 | tf_op jit(solution)/shard_map/all_to_all | solution.py:102
Sparse Core Ops, SparseCore 0:
  145.7 554.0 all-reduce.1
where the time goes:
time: 863 us; the launch traced here: 862 us
  waiting for transfers between devices  743 us (86%)
  starting transfers between devices  57.6 us (7%)
  matrix products  35.4 us (4%)
  between operations  14.4 us (2%)
    psum x1, waiting for transfers between devices, local(): density = lax.psum(partial_value, 'band')  554 us
    all_to_all x2, waiting for transfers between devices, local(): lax.all_to_all(stacked[member], 'slab', split_axis=2, concat_axis=1, tile...  92.9 us
    all_to_all x1, waiting for transfers between devices, local(): lax.all_to_all(jnp.stack((line_real, line_imag)), 'slab', split_axis=1, c...  48.5 us
    all_to_all x1, waiting for transfers between devices, local(): lax.all_to_all(jnp.stack((line_real, line_imag)), 'slab', split_axis=2, c...  47.4 us
    dot_general x36, matrix products, project(): return jnp.einsum(pattern, values, matrix, precision=lax.Precision.HIGHEST)  35.4 us
    all_to_all x1, starting transfers between devices, local(): lax.all_to_all(jnp.stack((line_real, line_imag)), 'slab', split_axis=1, c...  31.5 us
    all_to_all x2, starting transfers between devices, local(): lax.all_to_all(stacked[member], 'slab', split_axis=2, concat_axis=1, tile...  19.2 us
  transfers between devices with their start and end apart: 5, of which 5 were waited for; matrix products, arithmetic and copies ran while one was open for 1% of the time, Pallas kernels for 0%

commit v1 on v0

--- a/solution.py
+++ b/solution.py
@@ -82,7 +82,7 @@
             plane_real * plane_real + plane_imag * plane_imag
         )
     partial_value = partial_value * factor
-    density = lax.psum(partial_value, "band")
+    density = jnp.sum(lax.all_gather(partial_value, "band"), axis=0)
     own_density = lax.dynamic_slice_in_dim(density, band_index * band_rows, band_rows, 0)
     first_real = project("xyz,zw->xyw", density, cosine_table)
     first_imag = -project("xyz,zw->xyw", density, sine_table)

time: 863 us -> 723 us (0.84)
  the two profiles are of different devices: /device:TPU:65 before, /device:TPU:71 now
where the time goes in v1:
time: 723 us; the launch traced here: 714 us
  waiting for transfers between devices  612 us (85%)
  matrix products  34.5 us (5%)
  starting transfers between devices  34.5 us (5%)
  between operations  14.6 us (2%)
  other arithmetic  10.6 us (1%)
  local copies, waits for them, and re-layouts  8.38 us (1%)
    all_gather x1, waiting for transfers between devices, local(): density = jnp.sum(lax.all_gather(partial_value, 'band'), axis=0)  423 us
    all_to_all x2, waiting for transfers between devices, local(): lax.all_to_all(stacked[member], 'slab', split_axis=2, concat_axis=1, tile...  92.7 us
    all_to_all x1, waiting for transfers between devices, local(): lax.all_to_all(jnp.stack((line_real, line_imag)), 'slab', split_axis=1, c...  48.5 us
    all_to_all x1, waiting for transfers between devices, local(): lax.all_to_all(jnp.stack((line_real, line_imag)), 'slab', split_axis=2, c...  47.3 us
    dot_general x36, matrix products, project(): return jnp.einsum(pattern, values, matrix, precision=lax.Precision.HIGHEST)  34.5 us
    all_to_all x2, starting transfers between devices, local(): lax.all_to_all(stacked[member], 'slab', split_axis=2, concat_axis=1, tile...  19.2 us
  transfers between devices with their start and end apart: 5, of which 5 were waited for; matrix products, arithmetic and copies ran while one was open for 1% of the time, Pallas kernels for 0%

profile of v1, /device:TPU:71, one launch (start us, length us, event | category | flops | bytes accessed | tf_op | source)
XLA Modules:
  0.0 714.3 jit_solution(17745551562639735580)
XLA Ops:
  7.9 1.9 copy_multiply_fusion
  9.7 1.2 fusion.26
  12.2 1.2 convolution_subtract_fusion.1
  13.4 1.3 fusion.61
  14.7 1.3 fusion.64
  16.0 1.2 convolution_add_fusion.1
  17.2 1.3 fusion.1
  18.6 1.3 fusion
  20.1 1.6 copy.102
  21.7 12.5 %all-to-all-start = ((f32[2,8,128,128]{3,1,0,2:T(8,128)}), f32[2,8,128,128]{3,1,0,2:T(8,128)S(1)}, u32[]{:S(2)}, u32[]{:S(2)}) async-start(f32[2,8,128,128]{3,1,0,2:T(8,128)} %copy.102), calls=%async_computation | async-start | bytes 2097152 | tf_op jit(solution)/shard_map/all_to_all | solution.py:77
  34.2 1.6 copy.104
  35.8 47.0 %all-to-all-done = f32[2,8,128,128]{3,1,0,2:T(8,128)S(1)} async-done(((f32[2,8,128,128]{3,1,0,2:T(8,128)}), f32[2,8,128,128]{3,1,0,2:T(8,128)S(1)}, u32[]{:S(2)}, u32[]{:S(2)}) %all-to-all-start) | async-done | bytes 1048608 | tf_op jit(solution)/shard_map/all_to_all | solution.py:77
  82.7 6.7 all-to-all-start.1
  92.4 45.7 %all-to-all-done.1 = f32[2,8,128,128]{3,1,0,2:T(8,128)S(1)} async-done(((f32[2,8,128,128]{3,1,0,2:T(8,128)}), f32[2,8,128,128]{3,1,0,2:T(8,128)S(1)}, u32[]{:S(2)}, u32[]{:S(2)}) %all-to-all-start.1) | async-done | bytes 1048608 | tf_op jit(solution)/shard_map/all_to_all | solution.py:77
  141.6 1.6 fusion.19
  143.2 2.4 fusion.21
  145.6 423.3 %all-gather.3.cloned.1.call-done = f32[4096,8,128]{2,0,1:T(8,128)} async-done(((f32[128,8,128]{2,0,1:T(8,128)}), f32[4096,8,128]{2,0,1:T(8,128)}) %all-gather.3.cloned.1.call-update) | async-done | bytes 16777232 | tf_op jit(solution)/shard_map/all_gather | solution.py:85
  568.9 6.9 reduce_sum.9
  581.2 1.6 copy.108
  582.8 7.8 %all-to-all-start.2 = ((f32[2,128,8,128]{3,2,0,1:T(8,128)}), f32[2,128,8,128]{3,2,0,1:T(8,128)S(1)}, u32[]{:S(2)}, u32[]{:S(2)}) async-start(f32[2,128,8,128]{3,2,0,1:T(8,128)} %copy.108), calls=%async_computation.2 | async-start | bytes 2097152 | tf_op jit(solution)/shard_map/all_to_all | solution.py:92
  590.7 48.5 %all-to-all-done.2 = f32[2,128,8,128]{3,2,0,1:T(8,128)S(1)} async-done(((f32[2,128,8,128]{3,2,0,1:T(8,128)}), f32[2,128,8,128]{3,2,0,1:T(8,128)S(1)}, u32[]{:S(2)}, u32[]{:S(2)}) %all-to-all-start.2) | async-done | bytes 1048608 | tf_op jit(solution)/shard_map/all_to_all | solution.py:92
  646.4 1.6 copy.110
  648.0 7.0 all-to-all-start.3
  656.2 47.3 %all-to-all-done.3 = f32[2,8,128,128]{3,1,0,2:T(8,128)S(1)} async-done(((f32[2,8,128,128]{3,1,0,2:T(8,128)}), f32[2,8,128,128]{3,1,0,2:T(8,128)S(1)}, u32[]{:S(2)}, u32[]{:S(2)}) %all-to-all-start.3) | async-done | bytes 1048608 | tf_op jit(solution)/shard_map/all_to_all | solution.py:102
  (52 shorter events, 26.0 us)
Async XLA Ops:
  21.7 61.1 %all-to-all-start = ((f32[2,8,128,128]{3,1,0,2:T(8,128)}), f32[2,8,128,128]{3,1,0,2:T(8,128)S(1)}, u32[]{:S(2)}, u32[]{:S(2)}) async-start(f32[2,8,128,128]{3,1,0,2:T(8,128)} %copy.102), calls=%async_computation | async-start | bytes 2097152 | tf_op jit(solution)/shard_map/all_to_all | solution.py:77
  34.1 55.8 %copy-start.1 = (f32[2]{0:T(128)S(1)}, f32[2]{0:T(128)}, u32[]{:S(2)}) copy-start(f32[2]{0:T(128)} %param.6) | copy-start | bytes 28
  82.7 55.3 %all-to-all-start.1 = ((f32[2,8,128,128]{3,1,0,2:T(8,128)}), f32[2,8,128,128]{3,1,0,2:T(8,128)S(1)}, u32[]{:S(2)}, u32[]{:S(2)}) async-start(f32[2,8,128,128]{3,1,0,2:T(8,128)} %copy.104), calls=%async_computation.1 | async-start | bytes 2097152 | tf_op jit(solution)/shard_map/all_to_all | solution.py:77
  89.5 479.5 %all-gather.3.cloned.1.call-start = ((), (), s32[]{:S(2)}) async-start(), calls=%async_computation.4 | async-start | bytes 17301504 | tf_op jit(solution)/shard_map/all_gather | solution.py:85
  582.8 56.4 %all-to-all-start.2 = ((f32[2,128,8,128]{3,2,0,1:T(8,128)}), f32[2,128,8,128]{3,2,0,1:T(8,128)S(1)}, u32[]{:S(2)}, u32[]{:S(2)}) async-start(f32[2,128,8,128]{3,2,0,1:T(8,128)} %copy.108), calls=%async_computation.2 | async-start | bytes 2097152 | tf_op jit(solution)/shard_map/all_to_all | solution.py:92
  646.4 9.1 %copy-start = (f32[4,8,128]{2,1,0:T(8,128)S(1)}, f32[4,8,128]{2,1,0:T(8,128)}, u32[]{:S(2)}) copy-start(f32[4,8,128]{2,1,0:T(8,128)} %param.7) | copy-start | bytes 49156
  648.0 55.5 %all-to-all-start.3 = ((f32[2,8,128,128]{3,1,0,2:T(8,128)}), f32[2,8,128,128]{3,1,0,2:T(8,128)S(1)}, u32[]{:S(2)}, u32[]{:S(2)}) async-start(f32[2,8,128,128]{3,1,0,2:T(8,128)} %copy.110), calls=%async_computation.3 | async-start | bytes 2097152 | tf_op jit(solution)/shard_map/all_to_all | solution.py:102
Sparse Core Ops, SparseCore 0:
  145.7 423.1 all-gather.2
